TPU v7x, 32 devices: a whole 2x2x4 slice. The times are simulated.
32 devices in a mesh: groups: 2 (over x), tiles: 16 (over z, y, core).
Axes of the slice: x: 2, y: 2, z: 4, core: 2. Of those that a mesh axis runs over, the one named last changes fastest.
Arguments:
- coeffs: float32 [8192, 16384], P(('groups', 'tiles')), parts along dimension 0, may hold values from -0.09375 to 0.09375
- occupation: float32 [8192], P(('groups', 'tiles')), parts along dimension 0, may hold values from -1 to 1
- kept_tiles: int32 [64, 2], P('groups'), parts along dimension 0, may hold values from 0 to 255, as said below
- tile_slot: int32 [64], P('groups'), parts along dimension 0, may hold values from 0 to 31, as said below
- blocks: int32 [256, 8], P('groups'), parts along dimension 0, may hold values from 0 to 255, as said below
- batch_slot: int32 [256], P('groups'), parts along dimension 0, may hold values from 0 to 127, as said below
- tables: float32 [256, 512, 256], P(('groups', 'tiles')), parts along dimension 0, may hold values from -3.6 to 3.6
- weights: float32 [256, 256], P(('groups', 'tiles')), parts along dimension 0, may hold values from 0.005 to 0.05
- local_pot: float32 [256, 256], P(('groups', 'tiles')), parts along dimension 0, may hold values from -6 to 6
Outputs:
- density: float32 [256, 256], P(('groups', 'tiles')), parts along dimension 0
- matrix: float32 [64, 4096], P(('groups', 'tiles')), parts along dimension 0
There are 2 independent parts, one for each index of `groups`. A program takes and returns all parts, laid end to end along the dimension named above; each array names one. Nothing has to cross between parts.
Inputs may be any that keep to these rules, and one draw needn't show every extreme that they name: `kept_tiles`: distinct pairs (row block, column block). A permutation; slot tile_slot[k] is held by the device of index tile_slot[k] // 2 along tiles. Of the kept tiles that lie within the blocks of the batches held by one device, at most 2 are held by any one device. Each row names 8 different blocks. The devices come in aligned block clusters of 4 (indices 0 to 3, and so on); all batches held by the devices of one cluster name the same blocks, each batch in an order of its own, and different clusters name disjoint blocks. At most 16 kept tiles lie within the blocks of one batch. A permutation; the tables, weights, potential and density of batch b sit at slot batch_slot[b], held by the device of index batch_slot[b] // 8.
All inputs are finite; a program needn't handle non-finite values.
Results may differ from a plain program's by a relative error of at most 0.0003.
Values sent between devices are 32-bit elements; how exact they have to be, the bound alone decides.
No kernel may reach another device: no remote copies, remote signals or barrier semaphores. Data moves between devices by JAX's collectives and lax.ppermute only.
A program may use at most 128 MiB of HBM per device.

v0:
```python
import jax
import jax.numpy as jnp
from jax import lax
from jax.sharding import PartitionSpec as P

BS = 64
OV = 8


def body(coeffs, occupation, kept_tiles, tile_slot, blocks, batch_slot, tables, weights, local_pot):
    devices = lax.axis_size("tiles")
    my_index = lax.axis_index("tiles")
    kept_count = kept_tiles.shape[0]
    batch_count = tables.shape[0]
    batch_total = batch_slot.shape[0]
    state_count = coeffs.shape[0]
    block_total = coeffs.shape[1] // BS
    points = tables.shape[-1]
    width = OV * BS
    blocked = coeffs.reshape(state_count, block_total, BS)
    left_rows = jnp.take(blocked, kept_tiles[:, 0], axis=1)
    right_rows = jnp.take(blocked, kept_tiles[:, 1], axis=1) * occupation[:, None, None]
    partial = jnp.einsum(
        "srx,sry->rxy", left_rows, right_rows, precision=lax.Precision.HIGHEST
    ).reshape(kept_count, BS * BS)
    tile_values = lax.psum(partial, "tiles")
    ladder_batch = jnp.arange(batch_total, dtype=jnp.int32)
    slot_batch = jnp.zeros((batch_total,), jnp.int32).at[batch_slot].set(ladder_batch)
    my_batches = lax.dynamic_slice_in_dim(slot_batch, my_index * batch_count, batch_count)
    my_blocks = blocks[my_batches]
    canon = jnp.sort(my_blocks[0])
    ladder_ov = jnp.arange(OV, dtype=jnp.int32)
    match = my_blocks[:, :, None] == canon[None, None, :]
    source = jnp.sum(jnp.where(match, ladder_ov[None, :, None], 0), axis=1)
    grid = tables.reshape(batch_count, OV, BS, points)
    canon_tables = jnp.take_along_axis(grid, source[:, :, None, None], axis=1).reshape(
        batch_count, width, points
    )
    row_hit = kept_tiles[:, 0:1] == canon[None, :]
    col_hit = kept_tiles[:, 1:2] == canon[None, :]
    present = jnp.any(row_hit, axis=1) & jnp.any(col_hit, axis=1)
    row_place = jnp.sum(jnp.where(row_hit, ladder_ov[None, :], 0), axis=1)
    col_place = jnp.sum(jnp.where(col_hit, ladder_ov[None, :], 0), axis=1)
    kept_values = jnp.where(present[:, None], tile_values, 0.0).reshape(kept_count, BS, BS)
    dense = (
        jnp.zeros((OV, BS, OV, BS), jnp.float32)
        .at[row_place, :, col_place, :]
        .add(kept_values)
        .reshape(width, width)
    )
    mixed = jnp.einsum("uv,bvp->bup", dense, canon_tables, precision=lax.Precision.HIGH)
    density = jnp.sum(canon_tables * mixed, axis=1)
    potential = local_pot + density - density * density * density / 6.0
    weighted = canon_tables * (weights * potential)[:, None, :]
    full_matrix = jnp.einsum(
        "bup,bvp->uv", weighted, canon_tables, precision=lax.Precision.HIGH
    ).reshape(OV, BS, OV, BS)
    picked = full_matrix[row_place, :, col_place, :].reshape(kept_count, BS * BS)
    contrib = jnp.where(present[:, None], picked, 0.0)
    ladder_kept = jnp.arange(kept_count, dtype=jnp.int32)
    slot_kept = jnp.zeros((kept_count,), jnp.int32).at[tile_slot].set(ladder_kept)
    by_slot = contrib[slot_kept]
    matrix = lax.psum_scatter(by_slot, "tiles", scatter_dimension=0, tiled=True)
    return (density, matrix)


def solution(mesh):
    in_specs = (
        P(("groups", "tiles"), None),
        P(("groups", "tiles")),
        P("groups", None),
        P("groups"),
        P("groups", None),
        P("groups"),
        P(("groups", "tiles"), None, None),
        P(("groups", "tiles"), None),
        P(("groups", "tiles"), None),
    )
    out_specs = (P(("groups", "tiles"), None), P(("groups", "tiles"), None))
    return jax.shard_map(body, mesh=mesh, in_specs=in_specs, out_specs=out_specs, check_vma=False)
```

profile of v0, /device:TPU:1, one launch (start us, length us, event | category | flops | bytes accessed | tf_op | source)
XLA Modules:
  0.0 284.4 jit_solution(15538646823625262167)
XLA Ops:
  7.2 0.8 compare_and_fusion.2
  8.0 17.5 %copy.35 = f32[256,16384]{0,1:T(8,128)} copy(f32[256,16384]{1,0:T(8,128)} %param.11) | data formatting | bytes 33554432 | tf_op args[0]
  25.4 6.4 %gather_fusion.4 = f32[32,256,64]{1,2,0:T(8,128)S(1)} fusion(f32[256,256,64]{0,2,1:T(8,128)} %bitcast.76, s32[1024]{0:T(1024)S(1)} %get-tuple-element.23), kind=kCustom, calls=%fused_computation.clone | custom fusion | bytes 4194432 | tf_op jit(solution)/shard_map/jit(_take)/gather | solution.py:21
  31.9 7.8 %gather_fusion.5 = f32[32,256,64]{1,2,0:T(8,128)} fusion(f32[256,256,64]{0,2,1:T(8,128)} %bitcast.77, s32[1024]{0:T(1024)S(1)} %get-tuple-element.22), kind=kCustom, calls=%fused_computation.1.clone | custom fusion | bytes 4194432 | tf_op jit(solution)/shard_map/jit(_take)/gather | solution.py:22
  39.7 4.0 %fusion.5 = f32[32,64,64]{2,1,0:T(8,128)S(1)} fusion(f32[32,256,64]{1,2,0:T(8,128)} %gather_fusion.5, f32[32,256,64]{1,2,0:T(8,128)S(1)} %gather_fusion.4, f32[256]{0:T(256)S(1)} %copy-done.6, pred[32]{0:T(512)(128)(4,1)S(1)} %get-tuple-element.18, pred[32]{0:T(512)(128)(4,1)S(1)} %get-tuple-element.10), kind=kOutput, calls=%fused_computation.18 | convolution fusion | flops 404226048 | bytes 4719680 | tf_op jit(solution)/shard_map/srx,sry->rxy/dot_general | solution.py:23
  43.7 1.2 reshape.115
  45.1 1.0 scatter_custom_fusion
  46.2 0.6 gather_fusion
  46.8 1.0 sort.15
  48.2 0.9 scatter_custom_fusion.2
  49.0 5.0 %gather_fusion.3 = f32[64,64,256]{2,1,0:T(8,128)} fusion(f32[8,8,64,256]{3,2,1,0:T(8,128)} %bitcast.81, s32[64]{0:T(128)S(1)} %reshape.157), kind=kCustom, calls=%fused_computation.5 | custom fusion | bytes 8389120 | tf_op jit(solution)/shard_map/jit(take_along_axis)/gather | solution.py:36
  54.0 4.5 %broadcast_select_fusion = f32[8,8,64,256]{3,2,1,0:T(8,128)} fusion(f32[8,8,64,256]{3,2,1,0:T(8,128)} %bitcast.78, pred[8,8]{1,0:T(8,128)(4,1)S(1)} %compare_and_fusion), kind=kLoop, calls=%fused_computation.22 | loop fusion | flops 1048576 | bytes 8388672 | tf_op jit(solution)/shard_map/jit(take_along_axis)/select_n | solution.py:36
  58.5 5.4 %copy.34 = f32[8,512,256]{1,2,0:T(8,128)} copy(f32[8,512,256]{2,1,0:T(8,128)} %bitcast.79) | data formatting | bytes 8388608 | tf_op jit(solution)/shard_map/jit(take_along_axis)/gather | solution.py:36
  64.1 73.8 %all-reduce.4.cloned.1.call-done = f32[32,4096]{1,0:T(8,128)} async-done(((f32[32,4096]{1,0:T(8,128)}), f32[32,4096]{1,0:T(8,128)}) %all-reduce.4.cloned.1.call-update) | async-done | bytes 524304 | tf_op jit(solution)/shard_map/psum | solution.py:26
  137.9 1.1 broadcast_select_fusion.2
  139.1 0.4 reshape.173
  139.5 0.2 broadcast_in_dim.112
  139.7 2.4 scatter_fusion
  142.1 2.6 copy.36
  144.7 1.9 reshape.196
  146.7 10.2 %fusion.3 = f32[8,256]{1,0:T(8,128)S(1)} fusion(f32[8,512,256]{1,2,0:T(8,128)} %copy.34, f32[8,512,256]{2,1,0:T(8,128)} %bitcast.80, f32[512,512,1]{1,0,2:T(8,128)S(1)} %reshape.196, pred[8,512]{1,0:T(8,128)(4,1)S(1)} %broadcast_in_dim.107), kind=kOutput, calls=%fused_computation.13 | convolution fusion | flops 3224369152 | bytes 9449472 | tf_op jit(solution)/shard_map/uv,bvp->bup/dot_general | solution.py:51
  157.0 3.9 %multiply_bitcast_fusion = (f32[512,8,256]{0,2,1:T(8,128)}, f32[512,8,256]{0,2,1:T(8,128)}) fusion(f32[8,512,256]{1,2,0:T(8,128)S(1)} %copy-done, f32[8,256]{1,0:T(8,128)S(1)} %fusion.20, pred[8,512]{1,0:T(8,128)(4,1)S(1)} %broadcast_in_dim.107), kind=kLoop, calls=%fused_computation.15 | loop fusion | flops 2097152 | bytes 12595200 | tf_op jit(solution)/shard_map/bup,bvp->uv/dot_general | solution.py:55
  160.9 5.4 %copy.38 = f32[512,8,256]{2,1,0:T(8,128)} copy(f32[512,8,256]{0,2,1:T(8,128)} %get-tuple-element.14) | data formatting | bytes 8388608 | tf_op jit(solution)/shard_map/bup,bvp->uv/dot_general | solution.py:55
  166.4 5.4 %copy.39 = f32[512,8,256]{2,1,0:T(8,128)} copy(f32[512,8,256]{0,2,1:T(8,128)} %get-tuple-element.15) | data formatting | bytes 8388608 | tf_op jit(solution)/shard_map/bup,bvp->uv/dot_general | solution.py:55
  171.8 10.8 %fusion.9 = f32[8,64,8,64]{3,1,2,0:T(8,128)S(1)} fusion(f32[8,64,8,256]{3,2,1,0:T(8,128)} %bitcast.83, f32[8,64,8,256,1]{3,2,1,0,4:T(8,128)} %bitcast.82), kind=kOutput, calls=%fused_computation.23 | convolution fusion | flops 3221225472 | bytes 9437184 | tf_op jit(solution)/shard_map/bup,bvp->uv/dot_general | solution.py:55
  182.6 0.7 gather_fusion.1
  183.3 0.4 reshape.118
  183.7 0.1 broadcast_select_fusion.1
  183.8 1.5 gather_fusion.2
  185.3 0.6 dynamic-slice
  186.6 89.5 %all-reduce.6.cloned.1.call-done = f32[32,4096]{1,0:T(8,128)} async-done(((f32[32,4096]{1,0:T(8,128)}), f32[32,4096]{1,0:T(8,128)}) %all-reduce.6.cloned.1.call-update) | async-done | bytes 524304
  276.1 1.5 constant_dynamic-slice_fusion
  (48 shorter events, 0.9 us)
Async XLA Ops:
  7.2 130.8 %all-reduce.4.cloned.1.call-start = ((), (), s32[]{:S(2)}) async-start(), calls=%async_computation | async-start | bytes 1048576 | tf_op jit(solution)/shard_map/psum | solution.py:26
  31.9 7.8 %copy-start.6 = (f32[256]{0:T(256)S(1)}, f32[256]{0:T(256)}, u32[]{:S(2)}) copy-start(f32[256]{0:T(256)} %param.12) | copy-start | bytes 3076
  39.7 5.3 %copy-start.5 = (s32[32,2]{0,1:T(2,128)S(1)}, s32[32,2]{0,1:T(2,128)}, u32[]{:S(2)}) copy-start(s32[32,2]{0,1:T(2,128)} %param.13) | copy-start | bytes 772
  39.7 5.3 %copy-start.7 = (s32[128]{0:T(128)S(1)}, s32[128]{0:T(128)}, u32[]{:S(2)}) copy-start(s32[128]{0:T(128)} %param.16) | copy-start | bytes 1540
  39.7 6.4 %copy-start.4 = (s32[128,8]{0,1:T(8,128)S(1)}, s32[128,8]{0,1:T(8,128)}, u32[]{:S(2)}) copy-start(s32[128,8]{0,1:T(8,128)} %param.15) | copy-start | bytes 12292
  39.7 8.4 %copy-start.8 = (s32[32]{0:T(128)S(1)}, s32[32]{0:T(128)}, u32[]{:S(2)}) copy-start(s32[32]{0:T(128)} %param.14) | copy-start | bytes 388
  44.9 231.1 %all-reduce.6.cloned.1.call-start = ((), (), s32[]{:S(2)}) async-start(), calls=%async_computation.1 | async-start | bytes 1048576
  146.7 10.2 %copy-start.2 = (f32[8,256]{1,0:T(8,128)S(1)}, f32[8,256]{1,0:T(8,128)}, u32[]{:S(2)}) copy-start(f32[8,256]{1,0:T(8,128)} %param.18) | copy-start | bytes 24580
  146.7 10.2 %copy-start.3 = (f32[8,256]{1,0:T(8,128)S(1)}, f32[8,256]{1,0:T(8,128)}, u32[]{:S(2)}) copy-start(f32[8,256]{1,0:T(8,128)} %param.19) | copy-start | bytes 24580
  146.7 10.3 %copy-start = (f32[8,512,256]{1,2,0:T(8,128)S(1)}, f32[8,512,256]{1,2,0:T(8,128)}, u32[]{:S(2)}) copy-start(f32[8,512,256]{1,2,0:T(8,128)} %copy.34) | copy-start | bytes 12582916
  156.9 4.0 %copy-start.1 = (f32[8,256]{1,0:T(8,128)}, f32[8,256]{1,0:T(8,128)S(1)}, u32[]{:S(2)}) copy-start(f32[8,256]{1,0:T(8,128)S(1)} %fusion.3) | copy-start | bytes 24580
  183.3 2.0 copy-start.9
Sparse Core Ops, SparseCore 0:
  45.1 92.8 all-reduce.3
  185.4 90.5 all-reduce.5
where the time goes:
time: 285 us; the launch traced here: 284 us
  waiting for transfers between devices  163 us (57%)
  local copies, waits for them, and re-layouts  66.8 us (23%)
  matrix products  25 us (9%)
  between operations  15 us (5%)
  other arithmetic  14.2 us (5%)
    unnamed x3, waiting for transfers between devices  89.5 us
    psum x1, waiting for transfers between devices, body(): tile_values = lax.psum(partial, 'tiles')  73.8 us
    unnamed x24, local copies, waits for them, and re-layouts  19.7 us
    dot_general x2, local copies, waits for them, and re-layouts, body(): jnp.einsum('bup,bvp->uv', weighted, canon_tables, precision=lax.Precision...  10.9 us
    dot_general x1, matrix products, body(): jnp.einsum('bup,bvp->uv', weighted, canon_tables, precision=lax.Precision...  10.8 us
    gather x3, local copies, waits for them, and re-layouts, body(): jnp.take_along_axis(grid, source[:, :, None, None], axis=1)  10.4 us
    dot_general x1, matrix products, body(): jnp.einsum('uv,bvp->bup', dense, canon_tables, precision=lax.Precision.HIGH)  10.2 us
    gather x1, local copies, waits for them, and re-layouts, body(): jnp.take(blocked, kept_tiles[:, 1], axis=1) * occupation[:, None, None]  7.8 us
  transfers between devices with their start and end apart: 2, of which 2 were waited for; matrix products, arithmetic and copies ran while one was open for 7% of the time, Pallas kernels for 0%

commit v1 on v0

--- a/solution.py
+++ b/solution.py
@@ -23,7 +23,7 @@
     partial = jnp.einsum(
         "srx,sry->rxy", left_rows, right_rows, precision=lax.Precision.HIGHEST
     ).reshape(kept_count, BS * BS)
-    tile_values = lax.psum(partial, "tiles")
+    tile_values = jnp.sum(lax.all_gather(partial, "tiles"), axis=0)
     ladder_batch = jnp.arange(batch_total, dtype=jnp.int32)
     slot_batch = jnp.zeros((batch_total,), jnp.int32).at[batch_slot].set(ladder_batch)
     my_batches = lax.dynamic_slice_in_dim(slot_batch, my_index * batch_count, batch_count)

time: 285 us -> 271 us (0.951)
  waiting for transfers between devices: 163 us -> 146 us
  other arithmetic: 14.2 us -> 17.2 us
    psum x1 -> x0, waiting for transfers between devices: 73.8 us -> none  [body(): tile_values = lax.psum(partial, 'tiles')]
    all_gather x0 -> x1, waiting for transfers between devices: none -> 58.6 us  [body(): tile_values = jnp.sum(lax.all_gather(partial, 'tiles'), axis=0)]
    reduce_sum x0 -> x1, other arithmetic: none -> 3.83 us  [body(): tile_values = jnp.sum(lax.all_gather(partial, 'tiles'), axis=0)]
where the time goes in v1:
time: 271 us; the launch traced here: 270 us
  waiting for transfers between devices  146 us (54%)
  local copies, waits for them, and re-layouts  66.5 us (25%)
  matrix products  25 us (9%)
  other arithmetic  17.2 us (6%)
  between operations  15 us (6%)
    unnamed x3, waiting for transfers between devices  87.5 us
    all_gather x1, waiting for transfers between devices, body(): tile_values = jnp.sum(lax.all_gather(partial, 'tiles'), axis=0)  58.6 us
    unnamed x24, local copies, waits for them, and re-layouts  19.7 us
    dot_general x2, local copies, waits for them, and re-layouts, body(): jnp.einsum('bup,bvp->uv', weighted, canon_tables, precision=lax.Precision...  10.9 us
    dot_general x1, matrix products, body(): jnp.einsum('bup,bvp->uv', weighted, canon_tables, precision=lax.Precision...  10.8 us
    gather x3, local copies, waits for them, and re-layouts, body(): jnp.take_along_axis(grid, source[:, :, None, None], axis=1)  10.4 us
    dot_general x1, matrix products, body(): jnp.einsum('uv,bvp->bup', dense, canon_tables, precision=lax.Precision.HIGH)  10.2 us
    gather x1, local copies, waits for them, and re-layouts, body(): jnp.take(blocked, kept_tiles[:, 1], axis=1) * occupation[:, None, None]  7.8 us
  transfers between devices with their start and end apart: 2, of which 2 were waited for; matrix products, arithmetic and copies ran while one was open for 7% of the time, Pallas kernels for 0%

profile of v1, /device:TPU:1, one launch (start us, length us, event | category | flops | bytes accessed | tf_op | source)
XLA Modules:
  0.0 269.8 jit_solution(17676227348851934567)
XLA Ops:
  7.2 0.8 compare_and_fusion.2
  8.0 17.5 %copy.35 = f32[256,16384]{0,1:T(8,128)} copy(f32[256,16384]{1,0:T(8,128)} %param.11) | data formatting | bytes 33554432 | tf_op args[0]
  25.4 6.4 %gather_fusion.4 = f32[32,256,64]{1,2,0:T(8,128)S(1)} fusion(f32[256,256,64]{0,2,1:T(8,128)} %bitcast.76, s32[1024]{0:T(1024)S(1)} %get-tuple-element.23), kind=kCustom, calls=%fused_computation.clone | custom fusion | bytes 4194432 | tf_op jit(solution)/shard_map/jit(_take)/gather | solution.py:21
  31.9 7.8 %gather_fusion.5 = f32[32,256,64]{1,2,0:T(8,128)} fusion(f32[256,256,64]{0,2,1:T(8,128)} %bitcast.77, s32[1024]{0:T(1024)S(1)} %get-tuple-element.22), kind=kCustom, calls=%fused_computation.1.clone | custom fusion | bytes 4194432 | tf_op jit(solution)/shard_map/jit(_take)/gather | solution.py:22
  39.7 3.9 %fusion.5 = f32[32,64,64]{2,1,0:T(8,128)S(1)} fusion(f32[32,256,64]{1,2,0:T(8,128)} %gather_fusion.5, f32[32,256,64]{1,2,0:T(8,128)S(1)} %gather_fusion.4, f32[256]{0:T(256)S(1)} %copy-done.6, pred[32]{0:T(512)(128)(4,1)S(1)} %get-tuple-element.18, pred[32]{0:T(512)(128)(4,1)S(1)} %get-tuple-element.10), kind=kOutput, calls=%fused_computation.18 | convolution fusion | flops 404226048 | bytes 4719680 | tf_op jit(solution)/shard_map/srx,sry->rxy/dot_general | solution.py:23
  43.7 1.2 all_gather_reshape.3
  45.0 1.0 scatter_custom_fusion
  46.1 0.6 gather_fusion
  46.7 1.0 sort.15
  47.8 4.9 %gather_fusion.3 = f32[64,64,256]{2,1,0:T(8,128)} fusion(f32[8,8,64,256]{3,2,1,0:T(8,128)} %bitcast.81, s32[64]{0:T(128)S(1)} %reshape.156), kind=kCustom, calls=%fused_computation.5 | custom fusion | bytes 8389120 | tf_op jit(solution)/shard_map/jit(take_along_axis)/gather | solution.py:36
  52.8 5.4 %copy.34 = f32[8,512,256]{1,2,0:T(8,128)} copy(f32[8,512,256]{2,1,0:T(8,128)} %bitcast.78) | data formatting | bytes 8388608 | tf_op jit(solution)/shard_map/jit(take_along_axis)/gather | solution.py:36
  58.5 0.7 scatter_custom_fusion.2
  59.3 4.5 %broadcast_select_fusion = f32[8,8,64,256]{3,2,1,0:T(8,128)} fusion(f32[8,8,64,256]{3,2,1,0:T(8,128)} %bitcast.79, pred[8,8]{1,0:T(8,128)(4,1)S(1)} %compare_and_fusion), kind=kLoop, calls=%fused_computation.22 | loop fusion | flops 1048576 | bytes 8388672 | tf_op jit(solution)/shard_map/jit(take_along_axis)/select_n | solution.py:36
  63.9 58.6 %all-gather.2.cloned.1.call-done = f32[16,32,4096]{2,1,0:T(8,128)} async-done(((f32[1,32,4096]{2,1,0:T(8,128)}), f32[16,32,4096]{2,1,0:T(8,128)}) %all-gather.2.cloned.1.call-update) | async-done | bytes 8388624 | tf_op jit(solution)/shard_map/all_gather | solution.py:26
  122.4 3.8 %reduce_sum.59 = f32[32,4096]{1,0:T(8,128)S(1)} reduce(f32[16,32,4096]{2,1,0:T(8,128)} %all-gather.2.cloned.1.call-done, f32[]{:T(128)} %constant.10.clone.1), dimensions={0}, to_apply=%region_7.9 | reduce | flops 1966080 | bytes 8912900 | tf_op jit(solution)/shard_map/reduce_sum | solution.py:26
  126.3 0.4 reduce_sum.60
  126.7 0.1 broadcast_select_fusion.1
  126.8 0.2 broadcast_in_dim.116
  127.1 2.6 scatter_fusion
  129.7 2.5 copy.36
  132.2 1.9 reshape.195
  134.2 10.2 %fusion.3 = f32[8,256]{1,0:T(8,128)S(1)} fusion(f32[8,512,256]{1,2,0:T(8,128)} %copy.34, f32[8,512,256]{2,1,0:T(8,128)} %bitcast.80, f32[512,512,1]{1,0,2:T(8,128)S(1)} %reshape.195, pred[8,512]{1,0:T(8,128)(4,1)S(1)} %broadcast_in_dim.111), kind=kOutput, calls=%fused_computation.13 | convolution fusion | flops 3224369152 | bytes 9449472 | tf_op jit(solution)/shard_map/uv,bvp->bup/dot_general | solution.py:51
  144.4 3.9 %multiply_bitcast_fusion = (f32[512,8,256]{0,2,1:T(8,128)}, f32[512,8,256]{0,2,1:T(8,128)}) fusion(f32[8,512,256]{1,2,0:T(8,128)S(1)} %copy-done, f32[8,256]{1,0:T(8,128)S(1)} %fusion.20, pred[8,512]{1,0:T(8,128)(4,1)S(1)} %broadcast_in_dim.111), kind=kLoop, calls=%fused_computation.15 | loop fusion | flops 2097152 | bytes 12595200 | tf_op jit(solution)/shard_map/bup,bvp->uv/dot_general | solution.py:55
  148.4 5.4 %copy.38 = f32[512,8,256]{2,1,0:T(8,128)} copy(f32[512,8,256]{0,2,1:T(8,128)} %get-tuple-element.14) | data formatting | bytes 8388608 | tf_op jit(solution)/shard_map/bup,bvp->uv/dot_general | solution.py:55
  153.8 5.4 %copy.39 = f32[512,8,256]{2,1,0:T(8,128)} copy(f32[512,8,256]{0,2,1:T(8,128)} %get-tuple-element.15) | data formatting | bytes 8388608 | tf_op jit(solution)/shard_map/bup,bvp->uv/dot_general | solution.py:55
  159.3 10.8 %fusion.9 = f32[8,64,8,64]{3,1,2,0:T(8,128)S(1)} fusion(f32[8,64,8,256]{3,2,1,0:T(8,128)} %bitcast.83, f32[8,64,8,256,1]{3,2,1,0,4:T(8,128)} %bitcast.82), kind=kOutput, calls=%fused_computation.23 | convolution fusion | flops 3221225472 | bytes 9437184 | tf_op jit(solution)/shard_map/bup,bvp->uv/dot_general | solution.py:55
  170.1 0.7 gather_fusion.1
  170.8 0.4 reshape.117
  171.2 1.5 gather_fusion.2
  172.8 0.6 dynamic-slice
  174.0 87.4 %all-reduce.3.cloned.1.call-done = f32[32,4096]{1,0:T(8,128)} async-done(((f32[32,4096]{1,0:T(8,128)}), f32[32,4096]{1,0:T(8,128)}) %all-reduce.3.cloned.1.call-update) | async-done | bytes 524304
  261.5 1.5 constant_dynamic-slice_fusion
  (49 shorter events, 1.1 us)
Async XLA Ops:
  7.2 115.3 %all-gather.2.cloned.1.call-start = ((), (), s32[]{:S(2)}) async-start(), calls=%async_computation | async-start | bytes 8912896 | tf_op jit(solution)/shard_map/all_gather | solution.py:26
  31.9 7.8 %copy-start.6 = (f32[256]{0:T(256)S(1)}, f32[256]{0:T(256)}, u32[]{:S(2)}) copy-start(f32[256]{0:T(256)} %param.12) | copy-start | bytes 3076
  39.7 5.2 %copy-start.4 = (s32[128,8]{0,1:T(8,128)S(1)}, s32[128,8]{0,1:T(8,128)}, u32[]{:S(2)}) copy-start(s32[128,8]{0,1:T(8,128)} %param.15) | copy-start | bytes 12292
  39.7 5.3 %copy-start.7 = (s32[128]{0:T(128)S(1)}, s32[128]{0:T(128)}, u32[]{:S(2)}) copy-start(s32[128]{0:T(128)} %param.16) | copy-start | bytes 1540
  44.9 216.6 %all-reduce.3.cloned.1.call-start = ((), (), s32[]{:S(2)}) async-start(), calls=%async_computation.1 | async-start | bytes 1048576
  52.8 5.6 %copy-start.5 = (s32[32,2]{0,1:T(2,128)S(1)}, s32[32,2]{0,1:T(2,128)}, u32[]{:S(2)}) copy-start(s32[32,2]{0,1:T(2,128)} %param.13) | copy-start | bytes 772
  52.8 5.7 %copy-start.8 = (s32[32]{0:T(128)S(1)}, s32[32]{0:T(128)}, u32[]{:S(2)}) copy-start(s32[32]{0:T(128)} %param.14) | copy-start | bytes 388
  134.1 10.2 %copy-start.2 = (f32[8,256]{1,0:T(8,128)S(1)}, f32[8,256]{1,0:T(8,128)}, u32[]{:S(2)}) copy-start(f32[8,256]{1,0:T(8,128)} %param.18) | copy-start | bytes 24580
  134.2 10.2 %copy-start.3 = (f32[8,256]{1,0:T(8,128)S(1)}, f32[8,256]{1,0:T(8,128)}, u32[]{:S(2)}) copy-start(f32[8,256]{1,0:T(8,128)} %param.19) | copy-start | bytes 24580
  134.2 10.3 %copy-start = (f32[8,512,256]{1,2,0:T(8,128)S(1)}, f32[8,512,256]{1,2,0:T(8,128)}, u32[]{:S(2)}) copy-start(f32[8,512,256]{1,2,0:T(8,128)} %copy.34) | copy-start | bytes 12582916
  144.4 4.0 %copy-start.1 = (f32[8,256]{1,0:T(8,128)}, f32[8,256]{1,0:T(8,128)S(1)}, u32[]{:S(2)}) copy-start(f32[8,256]{1,0:T(8,128)S(1)} %fusion.3) | copy-start | bytes 24580
  170.8 2.0 copy-start.9
Sparse Core Ops, SparseCore 0:
  45.0 77.4 all-gather.1
  172.9 88.5 all-reduce.2
